TPU v7x, 256 devices: a whole 4x4x8 slice. The times are simulated.
256 devices in a mesh: shard: 64 (over y, z, core), cent: 4 (over x).
Axes of the slice: x: 4, y: 4, z: 8, core: 2. Of those that a mesh axis runs over, the one named last changes fastest.
Arguments:
- queries: bfloat16 [1024, 32, 128], P('shard'), may hold values from -6 to 6
- centroids: bfloat16 [196608, 128], P(('shard', 'cent')), may hold values from -0.5 to 0.5
- passages: bfloat16 [16384, 128, 128], P('shard', 'cent'), may hold values from -0.5 to 0.5
- lengths: int32 [16384], P('shard'), may hold values from 16 to 128, as said below
- passage_row: int32 [16384], replicated, may hold values from 0 to 16383, as said below
- candidates: int32 [1024, 16], P('shard'), may hold values from 0 to 16383, as said below
Outputs:
- token_best: float32 [1024, 32], P('shard')
- scores: float32 [1024, 16], P('shard')
Inputs may be any that keep to these rules, and one draw needn't show every extreme that they name: A permutation: passage g is stored at row passage_row[g]. The rows j < lengths[r] of stored passage r are real, the rest padding; the first stored passage of every index of shard has all 128. Among the 256 pairs of the queries of one index of shard, at most 12 have candidates stored at one owner (owner = passage_row[id] // 256); one owner takes exactly 12 pairs from every index of shard.
All inputs are finite; a program needn't handle non-finite values.
Results may differ from a plain program's by a relative error of at most 0.0003.
Values may be sent and summed in bfloat16 or wider, within the bound.
No kernel may reach another device: no remote copies, remote signals or barrier semaphores. Data moves between devices by JAX's collectives and lax.ppermute only.
A program may use at most 128 MiB of HBM per device.

v0:
```python
import jax
import jax.numpy as jnp
from jax import lax
from jax.sharding import PartitionSpec as P

masked_score = -1e30


def per_device(queries, centroids, passages, lengths, passage_row, candidates):
    query_count = queries.shape[0]
    query_tokens = queries.shape[1]
    feature_width = queries.shape[2]
    per_query = candidates.shape[1]
    passage_count = passages.shape[0]
    token_rows = passages.shape[1]
    shard_total = lax.axis_size("shard")
    capacity = max(2, 3 * query_count * per_query // shard_total)
    pairs_here = query_count * per_query
    my_shard = lax.axis_index("shard")
    query_block = lax.all_gather(queries, "shard", axis=0, tiled=True)
    cand_block = lax.all_gather(candidates, "shard", axis=0, tiled=True)
    flattened = query_block.reshape(-1, feature_width)
    scored = jnp.einsum("rd,cd->rc", flattened, centroids, preferred_element_type=jnp.float32)
    local_best = jnp.max(scored, axis=1).reshape(shard_total, query_count, query_tokens)
    gathered_best = lax.all_to_all(local_best, "shard", split_axis=0, concat_axis=0, tiled=True)
    shard_best = jnp.max(gathered_best, axis=0)
    all_rows = jnp.take(passage_row, cand_block.reshape(-1), axis=0)
    is_mine = (all_rows // passage_count == my_shard).reshape(shard_total, pairs_here)
    mine_int = is_mine.astype(jnp.int32)
    rank = jnp.cumsum(mine_int, axis=1) - mine_int
    source_ids = jnp.arange(shard_total, dtype=jnp.int32)[:, None]
    places = jnp.where(is_mine, source_ids * capacity + rank, shard_total * capacity).reshape(-1)
    pair_query = jnp.arange(shard_total * pairs_here, dtype=jnp.int32) // per_query
    slot_table = (
        jnp.zeros((shard_total * capacity,), jnp.int32)
        .at[places]
        .set(all_rows % passage_count, mode="drop")
    )
    query_table = (
        jnp.zeros((shard_total * capacity,), jnp.int32).at[places].set(pair_query, mode="drop")
    )
    asked = jnp.take(query_block, query_table, axis=0)
    chosen = jnp.take(passages, slot_table, axis=0)
    pair_scored = jnp.einsum("ntd,npd->ntp", asked, chosen, preferred_element_type=jnp.float32)
    token_index = lax.axis_index("cent") * token_rows + jnp.arange(token_rows, dtype=jnp.int32)
    valid_tokens = token_index[None, :] < jnp.take(lengths, slot_table, axis=0)[:, None]
    pair_scored = jnp.where(valid_tokens[:, None, :], pair_scored, masked_score)
    partial_value = jnp.max(pair_scored, axis=2)
    merged = lax.pmax(jnp.concatenate([shard_best, partial_value], axis=0), "cent")
    token_best = merged[:query_count]
    complete = merged[query_count:]
    pair_scores = (jnp.sum(complete, axis=1) / query_tokens).reshape(shard_total, capacity)
    returned = lax.all_to_all(pair_scores, "shard", split_axis=0, concat_axis=0, tiled=True)
    pair_rows = jnp.take(passage_row, candidates.reshape(-1), axis=0)
    owners = pair_rows // passage_count
    onehot = (owners[:, None] == jnp.arange(shard_total, dtype=jnp.int32)[None, :]).astype(
        jnp.int32
    )
    ranking = jnp.sum((jnp.cumsum(onehot, axis=0) - onehot) * onehot, axis=1)
    my_places = owners * capacity + ranking
    scores = jnp.take(returned.reshape(-1), my_places, axis=0).reshape(query_count, per_query)
    return (token_best, scores)


def solution(mesh):
    in_specs = (
        P("shard", None, None),
        P(("shard", "cent"), None),
        P("shard", "cent", None),
        P("shard"),
        P(),
        P("shard", None),
    )
    out_specs = (P("shard", None), P("shard", None))
    return jax.shard_map(
        per_device, mesh=mesh, in_specs=in_specs, out_specs=out_specs, check_vma=False
    )
```

profile of v0, /device:TPU:1, one launch (start us, length us, event | category | flops | bytes accessed | tf_op | source)
XLA Modules:
  0.0 415.2 jit_solution(12105765791642082866)
XLA Ops:
  7.9 0.8 reshape.445
  8.7 0.8 reshape.447
  9.5 0.8 reshape.446
  10.3 55.1 %all_gather.7 = s32[1024,16]{1,0:T(8,128)S(1)} all-gather(s32[16,16]{1,0:T(8,128)} %param.11), channel_id=1, replica_groups=mesh['shard'=64,'cent'=4] {'shard'}, dimensions={0}, use_global_device_ids=true | all-gather | bytes 66560 | tf_op jit(solution)/shard_map/all_gather | solution.py:21
  66.0 2.1 gather_fusion.4
  69.3 90.5 %gather_fusion = s32[16384]{0:T(1024)S(1)} fusion(s32[16384]{0:T(1024)S(1)} %copy-done.1, s32[16384]{0:T(1024)S(1)} %broadcast_clamp_fusion), kind=kCustom, calls=%fused_computation | custom fusion | bytes 196608 | tf_op jit(solution)/shard_map/jit(_take)/gather | solution.py:27
  161.5 60.3 %scatter_custom_fusion.1 = s32[768]{0:T(1024)S(1)} fusion(s32[16384]{0:T(1024)S(1)} %bitcast.49, s32[16384]{0:T(1024)S(1)} %add_select_fusion, s32[]{:T(128)} %constant.143.clone.1), kind=kCustom, calls=%fused_computation.97 | custom fusion | bytes 3076 | tf_op jit(solution)/shard_map/scatter | solution.py:40
  221.8 60.5 %scatter_custom_fusion = s32[768]{0:T(1024)S(1)} fusion(s32[16384]{0:T(1024)S(1)} %bitcast.50, s32[16384]{0:T(1024)S(1)} %add_select_fusion.1, s32[]{:T(128)} %constant.143.clone.1), kind=kCustom, calls=%fused_computation.99 | custom fusion | bytes 3076 | tf_op jit(solution)/shard_map/scatter | solution.py:37
  282.3 5.0 %gather_fusion.1 = s32[768]{0:T(1024)S(1)} fusion(s32[256]{0:T(256)S(1)} %copy-done.2, s32[1024]{0:T(1024)S(1)} %pad_clamp_fusion.3), kind=kCustom, calls=%fused_computation.1 | custom fusion | bytes 9216 | tf_op jit(solution)/shard_map/jit(_take)/gather | solution.py:46
  287.4 4.5 %gather_fusion.3 = bf16[768,32,128]{2,1,0:T(8,128)(2,1)} fusion(bf16[256,32,128]{2,1,0:T(8,128)(2,1)S(1)} %copy-done, s32[1024]{0:T(1024)S(1)} %pad_clamp_fusion.3), kind=kCustom, calls=%fused_computation.3 | custom fusion | bytes 12585984 | tf_op jit(solution)/shard_map/jit(_take)/gather | solution.py:43
  292.3 17.0 %convolution_reduce_fusion = f32[32768]{0:T(1024)S(1)} fusion(bf16[32768,128]{1,0:T(8,128)(2,1)} %bitcast.43, bf16[768,128]{1,0:T(8,128)(2,1)S(1)} %copy-done.5), kind=kOutput, calls=%fused_computation.8 | convolution fusion | flops 6467584000 | bytes 8716288 | tf_op jit(solution)/shard_map/rd,cd->rc/dot_general | solution.py:23
  309.5 0.9 reshape.532
  310.4 6.4 %all-to-all-start = ((f32[64,1,512]{2,1,0:T(1,128)}), f32[64,1,512]{2,1,0:T(1,128)S(1)}, u32[]{:S(2)}, u32[]{:S(2)}) async-start(f32[64,1,512]{2,1,0:T(1,128)} %reshape.532), calls=%async_computation | async-start | bytes 262144 | tf_op jit(solution)/shard_map/all_to_all | solution.py:25
  316.9 8.3 %gather_fusion.2 = bf16[768,32,128]{2,1,0:T(8,128)(2,1)} fusion(bf16[1024,32,128]{2,1,0:T(8,128)(2,1)} %all-gather.2.cloned.1.call-done, s32[1024]{0:T(1024)S(1)} %pad_clamp_fusion.2), kind=kCustom, calls=%fused_computation.2 | custom fusion | bytes 12585984 | tf_op jit(solution)/shard_map/jit(_take)/gather | solution.py:42
  325.2 8.3 %select_reduce_fusion = f32[768,32]{1,0:T(8,128)S(1)} fusion(pred[768,32]{1,0:T(8,128)(4,1)S(1)} %broadcast_compare_fusion, bf16[768,32,128]{2,1,0:T(8,128)(2,1)} %gather_fusion.3, pred[768]{0:T(1024)(128)(4,1)S(1)} %get-tuple-element.9, bf16[768,32,128]{2,1,0:T(8,128)(2,1)} %gather_fusion.2, pred[768]{0:T(1024)(128)(4,1)S(1)} %compare_and_fusion), kind=kOutput, calls=%fused_computation.9 | convolution fusion | flops 209166336 | bytes 12707328 | tf_op jit(solution)/shard_map/ntd,npd->ntp/dot_general | solution.py:44
  334.1 1.0 reduce.8
  335.4 0.7 pad_maximum_fusion
  336.2 44.7 %all-reduce.2.cloned.1.call-done = f32[784,32]{0,1:T(8,128)} async-done(((f32[784,32]{0,1:T(8,128)}), f32[784,32]{0,1:T(8,128)}) %all-reduce.2.cloned.1.call-update) | async-done | bytes 100368 | tf_op jit(solution)/shard_map/pmax | solution.py:49
  381.0 1.0 slice_reduce_fusion
  382.7 12.9 %all-to-all-start.1 = ((f32[64,1,12]{2,1,0:T(1,128)}), f32[64,1,12]{2,1,0:T(1,128)S(1)}, u32[]{:S(2)}, u32[]{:S(2)}) async-start(f32[64,1,12]{2,1,0:T(1,128)} %bitcast.9), calls=%async_computation.1 | async-start | bytes 65536 | tf_op jit(solution)/shard_map/all_to_all | solution.py:53
  395.7 0.7 slice.37
  397.1 7.7 %all-to-all-done.1 = f32[64,1,12]{2,1,0:T(1,128)S(1)} async-done(((f32[64,1,12]{2,1,0:T(1,128)}), f32[64,1,12]{2,1,0:T(1,128)S(1)}, u32[]{:S(2)}, u32[]{:S(2)}) %all-to-all-start.1) | async-done | bytes 3104 | tf_op jit(solution)/shard_map/all_to_all | solution.py:53
  405.4 0.7 reduce.7
  406.2 1.4 gather_fusion.5
  (72 shorter events, 8.6 us)
Async XLA Ops:
  7.2 280.2 %copy-start = (bf16[256,32,128]{2,1,0:T(8,128)(2,1)S(1)}, bf16[256,32,128]{2,1,0:T(8,128)(2,1)}, u32[]{:S(2)}) copy-start(bf16[256,32,128]{2,1,0:T(8,128)(2,1)} %param.8) | copy-start | bytes 6291460
  7.2 62.1 %copy-start.1 = (s32[16384]{0:T(1024)S(1)}, s32[16384]{0:T(1024)}, u32[]{:S(2)}) copy-start(s32[16384]{0:T(1024)} %param.10) | copy-start | bytes 196612
  7.2 285.1 %all-gather.2.cloned.1.call-start = ((), (), s32[]{:S(2)}) async-start(), calls=%async_computation.2 | async-start | bytes 8519680 | tf_op jit(solution)/shard_map/all_gather | solution.py:20
  69.0 90.8 %copy-start.4 = (s32[64,3]{0,1:T(4,128)}, s32[64,3]{0,1:T(4,128)S(1)}, u32[]{:S(2)}) copy-start(s32[64,3]{0,1:T(4,128)S(1)} %reduce-window.19) | copy-start | bytes 2308
  69.2 213.1 %copy-start.2 = (s32[256]{0:T(256)S(1)}, s32[256]{0:T(256)}, u32[]{:S(2)}) copy-start(s32[256]{0:T(256)} %param.9) | copy-start | bytes 3076
  287.3 4.6 %slice-start = ((s32[64,3]{0,1:T(4,128)}), s32[64,2]{0,1:T(2,128)S(1)}, s32[]{:S(2)}) async-start(s32[64,3]{0,1:T(4,128)} %copy-done.4), calls=%async_computation.4 | async-start | bytes 2048 | tf_op jit(solution)/shard_map/slice.5
  287.4 4.9 %copy-start.5 = (bf16[768,128]{1,0:T(8,128)(2,1)S(1)}, bf16[768,128]{1,0:T(8,128)(2,1)}, u32[]{:S(2)}) copy-start(bf16[768,128]{1,0:T(8,128)(2,1)} %param.7) | copy-start | bytes 589828
  310.4 23.2 %all-to-all-start = ((f32[64,1,512]{2,1,0:T(1,128)}), f32[64,1,512]{2,1,0:T(1,128)S(1)}, u32[]{:S(2)}, u32[]{:S(2)}) async-start(f32[64,1,512]{2,1,0:T(1,128)} %reshape.532), calls=%async_computation | async-start | bytes 262144 | tf_op jit(solution)/shard_map/all_to_all | solution.py:25
  316.8 64.1 %all-reduce.2.cloned.1.call-start = ((), (), s32[]{:S(2)}) async-start(), calls=%async_computation.3 | async-start | bytes 229376 | tf_op jit(solution)/shard_map/pmax | solution.py:49
  325.2 82.5 %copy-start.3 = (s32[16,16]{1,0:T(8,128)S(1)}, s32[16,16]{1,0:T(8,128)}, u32[]{:S(2)}) copy-start(s32[16,16]{1,0:T(8,128)} %param.11) | copy-start | bytes 3076
  382.7 22.2 %all-to-all-start.1 = ((f32[64,1,12]{2,1,0:T(1,128)}), f32[64,1,12]{2,1,0:T(1,128)S(1)}, u32[]{:S(2)}, u32[]{:S(2)}) async-start(f32[64,1,12]{2,1,0:T(1,128)} %bitcast.9), calls=%async_computation.1 | async-start | bytes 65536 | tf_op jit(solution)/shard_map/all_to_all | solution.py:53
Sparse Core Ops, SparseCore 0:
  10.8 87.3 all-gather.1
  336.3 44.5 all-reduce.1
where the time goes:
time: 416 us; the launch traced here: 415 us
  local copies, waits for them, and re-layouts  241 us (58%)
  blocking collectives  55.1 us (13%)
  waiting for transfers between devices  53.2 us (13%)
  matrix products  25.3 us (6%)
  starting transfers between devices  19.4 us (5%)
  between operations  14.4 us (3%)
  other arithmetic  6.63 us (2%)
    gather x1, local copies, waits for them, and re-layouts, per_device(): all_rows = jnp.take(passage_row, cand_block.reshape(-1), axis=0)  90.5 us
    scatter x1, local copies, waits for them, and re-layouts, per_device(): slot_table = jnp.zeros((shard_total * capacity,), jnp.int32).at[places].s...  60.5 us
    scatter x1, local copies, waits for them, and re-layouts, per_device(): jnp.zeros((shard_total * capacity,), jnp.int32).at[places]  60.3 us
    all_gather x1, blocking collectives, per_device(): cand_block = lax.all_gather(candidates, 'shard', axis=0, tiled=True)  55.1 us
    pmax x1, waiting for transfers between devices, per_device(): lax.pmax(jnp.concatenate([shard_best, partial_value], axis=0), 'cent')  44.7 us
    dot_general x1, matrix products, per_device(): jnp.einsum('rd,cd->rc', flattened, centroids, preferred_element_type=jnp....  17 us
    all_to_all x1, starting transfers between devices, per_device(): lax.all_to_all(pair_scores, 'shard', split_axis=0, concat_axis=0, tiled=T...  12.9 us
  transfers between devices with their start and end apart: 4, of which 2 were waited for; matrix products, arithmetic and copies ran while one was open for 60% of the time, Pallas kernels for 0%

commit v1 on v0

--- a/solution.py
+++ b/solution.py
@@ -4,6 +4,14 @@
 from jax.sharding import PartitionSpec as P
 
 masked_score = -1e30
+
+
+def gather_from_all(value, axis, dim):
+    peers = lax.axis_size(axis)
+    repeats = [peers if d == dim else 1 for d in range(value.ndim)]
+    return lax.all_to_all(
+        jnp.tile(value, repeats), axis, split_axis=dim, concat_axis=dim, tiled=True
+    )
 
 
 def per_device(queries, centroids, passages, lengths, passage_row, candidates):
@@ -18,7 +26,7 @@
     pairs_here = query_count * per_query
     my_shard = lax.axis_index("shard")
     query_block = lax.all_gather(queries, "shard", axis=0, tiled=True)
-    cand_block = lax.all_gather(candidates, "shard", axis=0, tiled=True)
+    cand_block = gather_from_all(candidates, "shard", 0)
     flattened = query_block.reshape(-1, feature_width)
     scored = jnp.einsum("rd,cd->rc", flattened, centroids, preferred_element_type=jnp.float32)
     local_best = jnp.max(scored, axis=1).reshape(shard_total, query_count, query_tokens)

time: 416 us -> 381 us (0.916)
  blocking collectives: 55.1 us -> 0 us
  starting transfers between devices: 19.4 us -> 32.3 us
  waiting for transfers between devices: 53.2 us -> 57.4 us
    all_gather x1 -> x0, blocking collectives: 55.1 us -> none  [per_device(): cand_block = lax.all_gather(candidates, 'shard', axis=0, tiled=True)]
    all_to_all x0 -> x1, starting transfers between devices: none -> 13.1 us  [gather_from_all(): lax.all_to_all(jnp.tile(value, repeats), axis, split_axis=dim, concat_axi...]
  transfers between devices with their start and end apart: 4 -> 5, of which waited for: 2 -> 3; matrix products, arithmetic and copies ran while one was open for 60% -> 66% of each run, Pallas kernels for 0% -> 0%
where the time goes in v1:
time: 381 us; the launch traced here: 380 us
  local copies, waits for them, and re-layouts  243 us (64%)
  waiting for transfers between devices  57.4 us (15%)
  starting transfers between devices  32.3 us (8%)
  matrix products  25.3 us (7%)
  between operations  14.4 us (4%)
  other arithmetic  7.43 us (2%)
    gather x1, local copies, waits for them, and re-layouts, per_device(): all_rows = jnp.take(passage_row, cand_block.reshape(-1), axis=0)  90.5 us
    scatter x1, local copies, waits for them, and re-layouts, per_device(): slot_table = jnp.zeros((shard_total * capacity,), jnp.int32).at[places].s...  60.5 us
    scatter x1, local copies, waits for them, and re-layouts, per_device(): jnp.zeros((shard_total * capacity,), jnp.int32).at[places]  60.3 us
    pmax x1, waiting for transfers between devices, per_device(): lax.pmax(jnp.concatenate([shard_best, partial_value], axis=0), 'cent')  44.7 us
    dot_general x1, matrix products, per_device(): jnp.einsum('rd,cd->rc', flattened, centroids, preferred_element_type=jnp....  17 us
    all_to_all x1, starting transfers between devices, gather_from_all(): lax.all_to_all(jnp.tile(value, repeats), axis, split_axis=dim, concat_axi...  13.1 us
    all_to_all x1, starting transfers between devices, per_device(): lax.all_to_all(pair_scores, 'shard', split_axis=0, concat_axis=0, tiled=T...  12.9 us
    gather x1, local copies, waits for them, and re-layouts, per_device(): asked = jnp.take(query_block, query_table, axis=0)  8.3 us
  transfers between devices with their start and end apart: 5, of which 3 were waited for; matrix products, arithmetic and copies ran while one was open for 66% of the time, Pallas kernels for 0%

profile of v1, /device:TPU:1, one launch (start us, length us, event | category | flops | bytes accessed | tf_op | source)
XLA Modules:
  0.0 380.3 jit_solution(4466139559782979723)
XLA Ops:
  8.7 0.9 reshape.543
  9.5 13.1 %all-to-all-start.1 = ((s32[64,1,256]{2,1,0:T(1,128)}), s32[64,1,256]{2,1,0:T(1,128)S(1)}, u32[]{:S(2)}, u32[]{:S(2)}) async-start(s32[64,1,256]{2,1,0:T(1,128)} %reshape.543), calls=%async_computation.1 | async-start | bytes 131072 | tf_op jit(solution)/shard_map/all_to_all | solution.py:12
  22.7 0.8 reshape.456
  23.5 0.8 reshape.458
  24.2 0.8 reshape.457
  25.0 2.1 gather_fusion.4
  28.3 4.2 %all-to-all-done.1 = s32[64,1,256]{2,1,0:T(1,128)S(1)} async-done(((s32[64,1,256]{2,1,0:T(1,128)}), s32[64,1,256]{2,1,0:T(1,128)S(1)}, u32[]{:S(2)}, u32[]{:S(2)}) %all-to-all-start.1) | async-done | bytes 65568 | tf_op jit(solution)/shard_map/all_to_all | solution.py:12
  32.9 0.8 reduce.8
  34.8 90.5 %gather_fusion = s32[16384]{0:T(1024)S(1)} fusion(s32[16384]{0:T(1024)S(1)} %copy-done.1, s32[16384]{0:T(1024)S(1)} %broadcast_clamp_fusion), kind=kCustom, calls=%fused_computation | custom fusion | bytes 196608 | tf_op jit(solution)/shard_map/jit(_take)/gather | solution.py:35
  127.0 60.3 %scatter_custom_fusion.1 = s32[768]{0:T(1024)S(1)} fusion(s32[16384]{0:T(1024)S(1)} %bitcast.51, s32[16384]{0:T(1024)S(1)} %add_select_fusion, s32[]{:T(128)} %constant.143.clone.1), kind=kCustom, calls=%fused_computation.97 | custom fusion | bytes 3076 | tf_op jit(solution)/shard_map/scatter | solution.py:48
  187.4 60.5 %scatter_custom_fusion = s32[768]{0:T(1024)S(1)} fusion(s32[16384]{0:T(1024)S(1)} %bitcast.52, s32[16384]{0:T(1024)S(1)} %add_select_fusion.1, s32[]{:T(128)} %constant.143.clone.1), kind=kCustom, calls=%fused_computation.99 | custom fusion | bytes 3076 | tf_op jit(solution)/shard_map/scatter | solution.py:45
  247.9 5.0 %gather_fusion.1 = s32[768]{0:T(1024)S(1)} fusion(s32[256]{0:T(256)S(1)} %copy-done.2, s32[1024]{0:T(1024)S(1)} %pad_clamp_fusion.3), kind=kCustom, calls=%fused_computation.1 | custom fusion | bytes 9216 | tf_op jit(solution)/shard_map/jit(_take)/gather | solution.py:54
  252.9 4.5 %gather_fusion.3 = bf16[768,32,128]{2,1,0:T(8,128)(2,1)} fusion(bf16[256,32,128]{2,1,0:T(8,128)(2,1)S(1)} %copy-done, s32[1024]{0:T(1024)S(1)} %pad_clamp_fusion.3), kind=kCustom, calls=%fused_computation.3 | custom fusion | bytes 12585984 | tf_op jit(solution)/shard_map/jit(_take)/gather | solution.py:51
  257.7 17.0 %convolution_reduce_fusion = f32[32768]{0:T(1024)S(1)} fusion(bf16[32768,128]{1,0:T(8,128)(2,1)} %bitcast.44, bf16[768,128]{1,0:T(8,128)(2,1)S(1)} %copy-done.4), kind=kOutput, calls=%fused_computation.8 | convolution fusion | flops 6467584000 | bytes 8716288 | tf_op jit(solution)/shard_map/rd,cd->rc/dot_general | solution.py:31
  274.9 0.9 reshape.545
  275.8 6.2 %all-to-all-start = ((f32[64,1,512]{2,1,0:T(1,128)}), f32[64,1,512]{2,1,0:T(1,128)S(1)}, u32[]{:S(2)}, u32[]{:S(2)}) async-start(f32[64,1,512]{2,1,0:T(1,128)} %reshape.545), calls=%async_computation | async-start | bytes 262144 | tf_op jit(solution)/shard_map/all_to_all | solution.py:33
  282.0 8.3 %gather_fusion.2 = bf16[768,32,128]{2,1,0:T(8,128)(2,1)} fusion(bf16[1024,32,128]{2,1,0:T(8,128)(2,1)} %all-gather.2.cloned.1.call-done, s32[1024]{0:T(1024)S(1)} %pad_clamp_fusion.2), kind=kCustom, calls=%fused_computation.2 | custom fusion | bytes 12585984 | tf_op jit(solution)/shard_map/jit(_take)/gather | solution.py:50
  290.3 8.3 %select_reduce_fusion = f32[768,32]{1,0:T(8,128)S(1)} fusion(pred[768,32]{1,0:T(8,128)(4,1)S(1)} %broadcast_compare_fusion, bf16[768,32,128]{2,1,0:T(8,128)(2,1)} %gather_fusion.3, pred[768]{0:T(1024)(128)(4,1)S(1)} %get-tuple-element.9, bf16[768,32,128]{2,1,0:T(8,128)(2,1)} %gather_fusion.2, pred[768]{0:T(1024)(128)(4,1)S(1)} %compare_and_fusion), kind=kOutput, calls=%fused_computation.9 | convolution fusion | flops 209166336 | bytes 12707328 | tf_op jit(solution)/shard_map/ntd,npd->ntp/dot_general | solution.py:52
  299.3 1.0 reduce.9
  301.4 44.7 %all-reduce.2.cloned.1.call-done = f32[784,32]{0,1:T(8,128)} async-done(((f32[784,32]{0,1:T(8,128)}), f32[784,32]{0,1:T(8,128)}) %all-reduce.2.cloned.1.call-update) | async-done | bytes 100368 | tf_op jit(solution)/shard_map/pmax | solution.py:57
  346.1 1.0 slice_reduce_fusion
  347.8 12.9 %all-to-all-start.2 = ((f32[64,1,12]{2,1,0:T(1,128)}), f32[64,1,12]{2,1,0:T(1,128)S(1)}, u32[]{:S(2)}, u32[]{:S(2)}) async-start(f32[64,1,12]{2,1,0:T(1,128)} %bitcast.10), calls=%async_computation.2 | async-start | bytes 65536 | tf_op jit(solution)/shard_map/all_to_all | solution.py:61
  362.3 7.7 %all-to-all-done.2 = f32[64,1,12]{2,1,0:T(1,128)S(1)} async-done(((f32[64,1,12]{2,1,0:T(1,128)}), f32[64,1,12]{2,1,0:T(1,128)S(1)}, u32[]{:S(2)}, u32[]{:S(2)}) %all-to-all-start.2) | async-done | bytes 3104 | tf_op jit(solution)/shard_map/all_to_all | solution.py:61
  371.4 1.4 gather_fusion.5
  (76 shorter events, 12.3 us)
Async XLA Ops:
  7.2 245.7 %copy-start = (bf16[256,32,128]{2,1,0:T(8,128)(2,1)S(1)}, bf16[256,32,128]{2,1,0:T(8,128)(2,1)}, u32[]{:S(2)}) copy-start(bf16[256,32,128]{2,1,0:T(8,128)(2,1)} %param.8) | copy-start | bytes 6291460
  7.2 27.6 %copy-start.1 = (s32[16384]{0:T(1024)S(1)}, s32[16384]{0:T(1024)}, u32[]{:S(2)}) copy-start(s32[16384]{0:T(1024)} %param.10) | copy-start | bytes 196612
  7.2 250.5 %all-gather.2.cloned.1.call-start = ((), (), s32[]{:S(2)}) async-start(), calls=%async_computation.3 | async-start | bytes 8519680 | tf_op jit(solution)/shard_map/all_gather | solution.py:28
  9.5 22.9 %all-to-all-start.1 = ((s32[64,1,256]{2,1,0:T(1,128)}), s32[64,1,256]{2,1,0:T(1,128)S(1)}, u32[]{:S(2)}, u32[]{:S(2)}) async-start(s32[64,1,256]{2,1,0:T(1,128)} %reshape.543), calls=%async_computation.1 | async-start | bytes 131072 | tf_op jit(solution)/shard_map/all_to_all | solution.py:12
  34.7 213.1 %copy-start.2 = (s32[256]{0:T(256)S(1)}, s32[256]{0:T(256)}, u32[]{:S(2)}) copy-start(s32[256]{0:T(256)} %param.9) | copy-start | bytes 3076
  252.9 4.8 %copy-start.4 = (bf16[768,128]{1,0:T(8,128)(2,1)S(1)}, bf16[768,128]{1,0:T(8,128)(2,1)}, u32[]{:S(2)}) copy-start(bf16[768,128]{1,0:T(8,128)(2,1)} %param.7) | copy-start | bytes 589828
  275.8 23.0 %all-to-all-start = ((f32[64,1,512]{2,1,0:T(1,128)}), f32[64,1,512]{2,1,0:T(1,128)S(1)}, u32[]{:S(2)}, u32[]{:S(2)}) async-start(f32[64,1,512]{2,1,0:T(1,128)} %reshape.545), calls=%async_computation | async-start | bytes 262144 | tf_op jit(solution)/shard_map/all_to_all | solution.py:33
  282.0 64.1 %all-reduce.2.cloned.1.call-start = ((), (), s32[]{:S(2)}) async-start(), calls=%async_computation.4 | async-start | bytes 229376 | tf_op jit(solution)/shard_map/pmax | solution.py:57
  290.3 82.5 %copy-start.3 = (s32[16,16]{1,0:T(8,128)S(1)}, s32[16,16]{1,0:T(8,128)}, u32[]{:S(2)}) copy-start(s32[16,16]{1,0:T(8,128)} %param.11) | copy-start | bytes 3076
  347.8 22.2 %all-to-all-start.2 = ((f32[64,1,12]{2,1,0:T(1,128)}), f32[64,1,12]{2,1,0:T(1,128)S(1)}, u32[]{:S(2)}, u32[]{:S(2)}) async-start(f32[64,1,12]{2,1,0:T(1,128)} %bitcast.10), calls=%async_computation.2 | async-start | bytes 65536 | tf_op jit(solution)/shard_map/all_to_all | solution.py:61
Sparse Core Ops, SparseCore 0:
  10.8 87.2 all-gather.1
  301.5 44.5 all-reduce.1
